TPU v7x, 512 devices: a whole 4x8x8 slice. The times are simulated.
512 devices in a mesh: fsdp: 64 (over y, x, core), tp: 8 (over z).
Axes of the slice: x: 4, y: 8, z: 8, core: 2. Of those that a mesh axis runs over, the one named last changes fastest.
Arguments:
- grads: bfloat16 [2, 12288, 2560], P(None, 'fsdp', 'tp'), may hold values from -16 to 16
- weights: float32 [2, 12288, 2560], P(None, 'fsdp', 'tp'), may hold values from -0.3 to 0.3
- basis: bfloat16 [2560, 2, 256], P('tp'), may hold values from -0.375 to 0.375
- first_moment: float32 [2, 12288, 256], P(None, 'fsdp', 'tp'), may hold values from -12 to 12
- second_moment: float32 [2, 12288, 256], P(None, 'fsdp', 'tp'), may hold values from 0.05 to 5
Outputs:
- weight_next: float32 [2, 12288, 2560], P(None, 'fsdp', 'tp')
- first_next: float32 [2, 12288, 256], P(None, 'fsdp', 'tp')
- second_next: float32 [2, 12288, 256], P(None, 'fsdp', 'tp')
- basis_next: bfloat16 [2560, 2, 256], P('tp')
All inputs are finite; a program needn't handle non-finite values.
Results may differ from a plain program's by a relative error of at most 0.0034.
Values may be sent and summed in bfloat16 or wider, within the bound.
No kernel may reach another device: no remote copies, remote signals or barrier semaphores. Data moves between devices by JAX's collectives and lax.ppermute only.
A program may use at most 64 MiB of HBM per device.

v0:
```python
import jax
import jax.numpy as jnp
from jax import lax
from jax.sharding import PartitionSpec as P

D = 2560
BETA_FIRST = 0.9
BETA_SECOND = 0.999
BIAS_FIRST = 0.9999734386011124
BIAS_SECOND = 0.0952078528862904
EPSILON = 1e-08
EPSILON_NORM = 1e-06
LEARNING_RATE = 0.1
GALORE_SCALE = 0.25


def adam_share(grad_share, first_moment, second_moment):
    first_next = BETA_FIRST * first_moment + (1.0 - BETA_FIRST) * grad_share
    second_next = BETA_SECOND * second_moment + (1.0 - BETA_SECOND) * grad_share * grad_share
    normal = first_next / BIAS_FIRST / (jnp.sqrt(second_next / BIAS_SECOND) + EPSILON)
    return (first_next, second_next, normal.astype(jnp.bfloat16))


def rebuild(image, sum_total, sum_cross):
    highest = lax.Precision.HIGHEST
    rank_width = image.shape[2]
    total = sum_total(jnp.sum(image * image, axis=(0, 2))) + EPSILON_NORM
    scaled = image * jnp.sqrt(rank_width / total)[None, :, None]
    cross = sum_cross(jnp.einsum("dmr,dms->mrs", scaled, scaled, precision=highest))
    shaped = 1.5 * scaled - 0.5 * jnp.einsum("dmr,mrs->dms", scaled, cross, precision=highest)
    return (jnp.sqrt(D / rank_width) * shaped).astype(jnp.bfloat16)


def shards(grads, weights, basis, first_moment, second_moment):
    projected_part = jnp.einsum("mfd,dmr->mfr", grads, basis, preferred_element_type=jnp.float32)
    summed_share = lax.psum_scatter(projected_part, "tp", scatter_dimension=2, tiled=True)
    first_next, second_next, normal_half = adam_share(summed_share, first_moment, second_moment)
    projected_half, normal_full = (
        lax.all_gather(summed_share.astype(jnp.bfloat16), "tp", axis=2, tiled=True),
        lax.all_gather(normal_half, "tp", axis=2, tiled=True),
    )
    update = jnp.einsum("mfr,dmr->mfd", normal_full, basis, preferred_element_type=jnp.float32)
    weight_next = weights - LEARNING_RATE * GALORE_SCALE * update

    def block_total(value):
        return lax.psum(value, "tp")

    def block_gram(value):
        return lax.psum(value, "tp")

    image = lax.psum(
        jnp.einsum("mfd,mfr->dmr", grads, projected_half, preferred_element_type=jnp.float32),
        "fsdp",
    )
    basis_next = rebuild(image, block_total, block_gram)
    return (weight_next, first_next, second_next, basis_next)


def solution(mesh):
    in_specs = (
        P(None, "fsdp", "tp"),
        P(None, "fsdp", "tp"),
        P("tp", None, None),
        P(None, "fsdp", "tp"),
        P(None, "fsdp", "tp"),
    )
    out_specs = (
        P(None, "fsdp", "tp"),
        P(None, "fsdp", "tp"),
        P(None, "fsdp", "tp"),
        P("tp", None, None),
    )
    return jax.shard_map(shards, mesh=mesh, in_specs=in_specs, out_specs=out_specs, check_vma=False)
```

profile of v0, /device:TPU:2, one launch (start us, length us, event | category | flops | bytes accessed | tf_op | source)
XLA Modules:
  0.0 383.9 jit_solution(17990277985158223660)
XLA Ops:
  7.2 0.0 copy-start
  7.2 0.0 reduce-scatter.2.cloned.1.call-start
  7.2 0.9 copy-done
  8.1 2.1 fusion.11
  10.2 0.0 copy-start.4
  10.2 0.0 copy-start.5
  10.2 0.0 reduce-scatter.2.cloned.1.call-update
  10.3 0.0 copy-start.2
  10.3 0.0 all-reduce.3.cloned.1.call-start
  10.3 46.8 %reduce-scatter.2.cloned.1.call-done = f32[2,192,32]{1,2,0:T(8,128)} async-done(((f32[2,192,256]{1,2,0:T(8,128)}), f32[2,192,32]{1,2,0:T(8,128)}) %reduce-scatter.2.cloned.1.call-update) | async-done | bytes 49168 | tf_op jit(solution)/shard_map/reduce_scatter | solution.py:36
  57.2 0.0 copy-done.4
  57.2 0.0 copy-done.5
  57.2 1.6 divide_convert_fusion
  58.8 24.8 %all_gather.7 = bf16[2,192,256]{1,2,0:T(8,128)(2,1)S(1)} all-gather(bf16[2,192,32]{1,2,0:T(8,128)(2,1)S(1)} %get-tuple-element.11), channel_id=1, replica_groups=mesh['fsdp'=64,'tp'=8] {'tp'}, dimensions={2}, use_global_device_ids=true | all-gather | bytes 221184 | tf_op jit(solution)/shard_map/all_gather | solution.py:39
  83.6 0.0 copy-done.2
  83.6 1.2 convolution_bitcast_fusion
  84.7 0.0 all-reduce.3.cloned.1.call-update
  84.8 0.0 all-reduce.5.cloned.1.call-start
  84.8 192.2 %all-reduce.3.cloned.1.call-done = f32[320,2,256]{2,0,1:T(8,128)} async-done(((f32[320,2,256]{2,0,1:T(8,128)}), f32[320,2,256]{2,0,1:T(8,128)}) %all-reduce.3.cloned.1.call-update) | async-done | bytes 655376 | tf_op jit(solution)/shard_map/psum | solution.py:51
  277.0 0.0 copy-start.1
  277.0 1.3 multiply_reduce_fusion
  278.3 18.1 %psum.22 = f32[2]{0:T(128)S(1)} all-reduce(f32[2]{0:T(128)S(1)} %multiply_reduce_fusion), channel_id=1, replica_groups=mesh['fsdp'=64,'tp'=8] {'tp'}, use_global_device_ids=true, to_apply=%region_3.0 | all-reduce | flops 2 | bytes 16 | tf_op jit(solution)/shard_map/psum | solution.py:46
  296.4 0.0 copy-done.1
  296.4 2.4 fusion.5
  298.8 0.0 copy-start.3
  298.8 0.0 all-reduce.5.cloned.1.call-update
  298.8 25.0 %all_gather.6 = bf16[2,192,256]{1,2,0:T(8,128)(2,1)S(1)} all-gather(bf16[2,192,32]{1,2,0:T(8,128)(2,1)S(1)} %get-tuple-element.8), channel_id=1, replica_groups=mesh['fsdp'=64,'tp'=8] {'tp'}, dimensions={2}, use_global_device_ids=true | all-gather | bytes 221184 | tf_op jit(solution)/shard_map/all_gather | solution.py:40
  323.9 0.0 copy-done.3
  323.9 1.2 fusion.3
  325.0 49.4 %all-reduce.5.cloned.1.call-done = f32[2,256,256]{2,1,0:T(8,128)} async-done(((f32[2,256,256]{2,1,0:T(8,128)}), f32[2,256,256]{2,1,0:T(8,128)}) %all-reduce.5.cloned.1.call-update) | async-done | bytes 524304 | tf_op jit(solution)/shard_map/psum | solution.py:49
  374.4 1.9 fusion.4
  376.3 1.1 copy.11
  (1 shorter events, 0.0 us)
Async XLA Ops:
  7.2 1.0 copy-start
  7.2 50.0 %reduce-scatter.2.cloned.1.call-start = ((), (), s32[]{:S(2)}) async-start(), calls=%async_computation.1 | async-start | bytes 589824 | tf_op jit(solution)/shard_map/reduce_scatter | solution.py:36
  10.2 46.9 %copy-start.4 = (f32[2,192,32]{1,2,0:T(8,128)S(1)}, f32[2,192,32]{1,2,0:T(8,128)}, u32[]{:S(2)}) copy-start(f32[2,192,32]{1,2,0:T(8,128)} %param.8) | copy-start | bytes 147460
  10.2 46.9 %copy-start.5 = (f32[2,192,32]{1,2,0:T(8,128)S(1)}, f32[2,192,32]{1,2,0:T(8,128)}, u32[]{:S(2)}) copy-start(f32[2,192,32]{1,2,0:T(8,128)} %param.9) | copy-start | bytes 147460
  10.3 73.3 %copy-start.2 = (bf16[2,192,320]{2,1,0:T(8,128)(2,1)S(1)}, bf16[2,192,320]{2,1,0:T(8,128)(2,1)}, u32[]{:S(2)}) copy-start(bf16[2,192,320]{2,1,0:T(8,128)(2,1)} %param.5) | copy-start | bytes 737284
  10.3 266.7 %all-reduce.3.cloned.1.call-start = ((), (), s32[]{:S(2)}) async-start(), calls=%async_computation.2 | async-start | bytes 1310720 | tf_op jit(solution)/shard_map/psum | solution.py:51
  84.8 289.6 %all-reduce.5.cloned.1.call-start = ((), (), s32[]{:S(2)}) async-start(), calls=%async_computation.3 | async-start | bytes 1048576 | tf_op jit(solution)/shard_map/psum | solution.py:49
  277.0 19.4 %copy-start.1 = (f32[320,2,256]{2,0,1:T(8,128)S(1)}, f32[320,2,256]{2,0,1:T(8,128)}, u32[]{:S(2)}) copy-start(f32[320,2,256]{2,0,1:T(8,128)} %all-reduce.3.cloned.1.call-done) | copy-start | bytes 1966084
  298.8 25.0 %copy-start.3 = (f32[2,192,320]{2,1,0:T(8,128)S(1)}, f32[2,192,320]{2,1,0:T(8,128)}, u32[]{:S(2)}) copy-start(f32[2,192,320]{2,1,0:T(8,128)} %param.6) | copy-start | bytes 1474564
Sparse Core Ops, SparseCore 0:
  11.4 45.7 reduce-scatter.1
  84.9 192.0 all-reduce.2
  299.0 75.3 all-reduce.4
where the time goes:
time: 384 us
  waiting for transfers between devices  288 us (75%)
  blocking collectives  67.9 us (18%)
  between operations  13.8 us (4%)
  matrix products  8.7 us (2%)
    psum x1, waiting for transfers between devices, shards(): lax.psum(jnp.einsum('mfd,mfr->dmr', grads, projected_half, preferred_elem...  192 us
    psum x1, waiting for transfers between devices, block_gram(): return lax.psum(value, 'tp')  49.4 us
    reduce_scatter x1, waiting for transfers between devices, shards(): lax.psum_scatter(projected_part, 'tp', scatter_dimension=2, tiled=True)  46.8 us
    all_gather x1, blocking collectives, shards(): lax.all_gather(normal_half, 'tp', axis=2, tiled=True)  25 us
    all_gather x1, blocking collectives, shards(): lax.all_gather(summed_share.astype(jnp.bfloat16), 'tp', axis=2, tiled=True)  24.8 us
    psum x1, blocking collectives, block_total(): return lax.psum(value, 'tp')  18.1 us
  transfers between devices with their start and end apart: 3, of which 3 were waited for; matrix products, arithmetic and copies ran while one was open for 0% of the time, Pallas kernels for 0%

commit v1 on v0

--- a/solution.py
+++ b/solution.py
@@ -48,9 +48,12 @@
     def block_gram(value):
         return lax.psum(value, "tp")
 
-    image = lax.psum(
-        jnp.einsum("mfd,mfr->dmr", grads, projected_half, preferred_element_type=jnp.float32),
-        "fsdp",
+    image = jnp.sum(
+        lax.all_gather(
+            jnp.einsum("mfd,mfr->dmr", grads, projected_half, preferred_element_type=jnp.float32),
+            "fsdp",
+        ),
+        axis=0,
     )
     basis_next = rebuild(image, block_total, block_gram)
     return (weight_next, first_next, second_next, basis_next)

time: 384 us -> 372 us (0.969)
  waiting for transfers between devices: 288 us -> 262 us
  other arithmetic: 2.95 us -> 16.4 us
    psum x1 -> x0, waiting for transfers between devices: 192 us -> none  [shards(): lax.psum(jnp.einsum('mfd,mfr->dmr', grads, projected_half, preferred_elem...]
    all_gather x0 -> x1, waiting for transfers between devices: none -> 165 us  [shards(): lax.all_gather(jnp.einsum('mfd,mfr->dmr', grads, projected_half, preferre...]
    reduce_sum x0 -> x1, other arithmetic: none -> 14.6 us  [shards(): jnp.sum(lax.all_gather(jnp.einsum('mfd,mfr->dmr', grads, projected_half,...]
where the time goes in v1:
time: 372 us
  waiting for transfers between devices  262 us (70%)
  blocking collectives  67.9 us (18%)
  other arithmetic  16.4 us (4%)
  between operations  13.8 us (4%)
  matrix products  9.7 us (3%)
    all_gather x1, waiting for transfers between devices, shards(): lax.all_gather(jnp.einsum('mfd,mfr->dmr', grads, projected_half, preferre...  165 us
    psum x1, waiting for transfers between devices, block_gram(): return lax.psum(value, 'tp')  49.5 us
    reduce_scatter x1, waiting for transfers between devices, shards(): lax.psum_scatter(projected_part, 'tp', scatter_dimension=2, tiled=True)  46.9 us
    all_gather x1, blocking collectives, shards(): lax.all_gather(normal_half, 'tp', axis=2, tiled=True)  25 us
    all_gather x1, blocking collectives, shards(): lax.all_gather(summed_share.astype(jnp.bfloat16), 'tp', axis=2, tiled=True)  24.8 us
    psum x1, blocking collectives, block_total(): return lax.psum(value, 'tp')  18.1 us
    reduce_sum x1, other arithmetic, shards(): jnp.sum(lax.all_gather(jnp.einsum('mfd,mfr->dmr', grads, projected_half,...  14.6 us
  transfers between devices with their start and end apart: 3, of which 3 were waited for; matrix products, arithmetic and copies ran while one was open for 0% of the time, Pallas kernels for 0%

profile of v1, /device:TPU:2, one launch (start us, length us, event | category | flops | bytes accessed | tf_op | source)
XLA Modules:
  0.0 371.5 jit_solution(6253818184470670349)
XLA Ops:
  7.2 0.0 copy-start
  7.2 0.0 copy-start.1
  7.2 0.0 reduce-scatter.2.cloned.1.call-start
  7.2 0.9 copy-done
  8.1 2.1 fusion.11
  10.2 0.0 reduce-scatter.2.cloned.1.call-update
  10.3 0.0 all-gather.3.cloned.1.call-start
  10.3 46.9 %reduce-scatter.2.cloned.1.call-done = f32[2,192,32]{1,2,0:T(8,128)} async-done(((f32[2,192,256]{1,2,0:T(8,128)}), f32[2,192,32]{1,2,0:T(8,128)}) %reduce-scatter.2.cloned.1.call-update) | async-done | bytes 49168 | tf_op jit(solution)/shard_map/reduce_scatter | solution.py:36
  57.2 1.6 divide_convert_fusion
  58.8 24.8 %all_gather.13 = bf16[2,192,256]{1,2,0:T(8,128)(2,1)S(1)} all-gather(bf16[2,192,32]{1,2,0:T(8,128)(2,1)S(1)} %get-tuple-element.11), channel_id=1, replica_groups=mesh['fsdp'=64,'tp'=8] {'tp'}, dimensions={2}, use_global_device_ids=true | all-gather | bytes 221184 | tf_op jit(solution)/shard_map/all_gather | solution.py:39
  83.6 2.1 convolution_bitcast_fusion
  85.7 0.0 all-gather.3.cloned.1.call-update
  85.8 0.0 all-reduce.2.cloned.1.call-start
  85.8 165.2 %all-gather.3.cloned.1.call-done = f32[20480,2,256]{2,0,1:T(8,128)} async-done(((f32[320,2,256]{2,0,1:T(8,128)}), f32[20480,2,256]{2,0,1:T(8,128)}) %all-gather.3.cloned.1.call-update) | async-done | bytes 41943056 | tf_op jit(solution)/shard_map/all_gather | solution.py:52
  251.0 14.6 %reduce_sum.18 = f32[320,2,256]{2,0,1:T(8,128)S(1)} reduce(f32[64,320,2,256]{3,1,0,2:T(8,128)} %bitcast.16, f32[]{:T(128)} %constant.10.clone.1), dimensions={0}, to_apply=%region_1.0 | reduce | flops 10321920 | bytes 42598404 | tf_op jit(solution)/shard_map/reduce_sum | solution.py:51
  265.6 0.2 multiply_reduce_fusion
  265.8 18.1 %psum.14 = f32[2]{0:T(128)S(1)} all-reduce(f32[2]{0:T(128)S(1)} %multiply_reduce_fusion), channel_id=1, replica_groups=mesh['fsdp'=64,'tp'=8] {'tp'}, use_global_device_ids=true, to_apply=%region_3.0 | all-reduce | flops 2 | bytes 16 | tf_op jit(solution)/shard_map/psum | solution.py:46
  283.9 2.4 fusion.5
  286.3 0.0 all-reduce.2.cloned.1.call-update
  286.4 25.0 %all_gather.12 = bf16[2,192,256]{1,2,0:T(8,128)(2,1)S(1)} all-gather(bf16[2,192,32]{1,2,0:T(8,128)(2,1)S(1)} %get-tuple-element.8), channel_id=1, replica_groups=mesh['fsdp'=64,'tp'=8] {'tp'}, dimensions={2}, use_global_device_ids=true | all-gather | bytes 221184 | tf_op jit(solution)/shard_map/all_gather | solution.py:40
  311.4 0.0 copy-done.1
  311.4 1.2 fusion.3
  312.6 49.5 %all-reduce.2.cloned.1.call-done = f32[2,256,256]{2,1,0:T(8,128)} async-done(((f32[2,256,256]{2,1,0:T(8,128)}), f32[2,256,256]{2,1,0:T(8,128)}) %all-reduce.2.cloned.1.call-update) | async-done | bytes 524304 | tf_op jit(solution)/shard_map/psum | solution.py:49
  362.0 1.9 fusion.4
  363.9 1.1 copy.11
  (1 shorter events, 0.0 us)
Async XLA Ops:
  7.2 1.0 copy-start
  7.2 304.2 %copy-start.1 = (f32[2,192,320]{2,1,0:T(8,128)S(1)}, f32[2,192,320]{2,1,0:T(8,128)}, u32[]{:S(2)}) copy-start(f32[2,192,320]{2,1,0:T(8,128)} %param.6) | copy-start | bytes 1474564
  7.2 50.0 %reduce-scatter.2.cloned.1.call-start = ((), (), s32[]{:S(2)}) async-start(), calls=%async_computation.1 | async-start | bytes 589824 | tf_op jit(solution)/shard_map/reduce_scatter | solution.py:36
  10.3 240.8 %all-gather.3.cloned.1.call-start = ((), (), s32[]{:S(2)}) async-start(), calls=%async_computation.3 | async-start | bytes 42598400 | tf_op jit(solution)/shard_map/all_gather | solution.py:52
  85.8 276.3 %all-reduce.2.cloned.1.call-start = ((), (), s32[]{:S(2)}) async-start(), calls=%async_computation.2 | async-start | bytes 1048576 | tf_op jit(solution)/shard_map/psum | solution.py:49
Sparse Core Ops, SparseCore 0:
  11.4 45.7 reduce-scatter.1
  85.9 165.1 all-gather.2
  286.5 75.4 all-reduce.1
